TPU v7x, 32 devices: a whole 2x2x4 slice. The times are simulated.
32 devices in a mesh: layer: 4 (over y, x), tok: 8 (over z, core).
Axes of the slice: x: 2, y: 2, z: 4, core: 2. Of those that a mesh axis runs over, the one named last changes fastest.
Arguments:
- residual: bfloat16 [4, 1024, 3584], P('layer', 'tok'), may hold values from -6 to 6
- targets: bfloat16 [4, 1024, 3584], P('layer', 'tok'), may hold values from -6 to 6
- block_ids: int32 [4, 1024, 2], P(None, 'tok'), may hold values from 0 to 127, all different within a row; in each aligned block of 128 rows (0 to 127, 128 to 255, ..., all dimensions but the last counted through in order) at most 4 rows name the same one
- encoder_weight: bfloat16 [4, 3584, 16384], P('layer', None, 'tok'), may hold values from -0.09375 to 0.09375
- encoder_bias: float32 [4, 16384], P('layer', 'tok'), may hold values from -3 to 3
- decoder_weight: bfloat16 [4, 4, 16384, 3584], P('layer', None, 'tok'), may hold values from -0.25 to 0.25
- decoder_bias: float32 [4, 3584], P('layer'), may hold values from -3 to 3
Outputs:
- reconstruction: bfloat16 [4, 1024, 3584], P('layer', 'tok')
- error: float32 [4, 1024], P('layer', 'tok')
Inputs may be any that keep to these rules, and one draw needn't show every extreme that they name: `block_ids`: A token's 2 blocks in a layer are distinct. In each layer, the 128 rows of one device (aligned blocks of tokens) name no block more than 4 times, and some block exactly 4 times.
All inputs are finite; a program needn't handle non-finite values.
Results may differ from a plain program's by a relative error of at most 0.0053.
Values may be sent and summed in bfloat16 or wider, within the bound.
No kernel may reach another device: no remote copies, remote signals or barrier semaphores. Data moves between devices by JAX's collectives and lax.ppermute only.
A program may use at most 192 MiB of HBM per device.

v0:
```python
import jax
import jax.numpy as jnp
from jax import lax
from jax.sharding import PartitionSpec as P

BLOCK = 128


def slot_positions(ids, blocks, capacity):
    flat_ids = ids.reshape(-1)
    onehot = (flat_ids[:, None] == jnp.arange(blocks, dtype=jnp.int32)[None, :]).astype(jnp.int32)
    before = jnp.cumsum(onehot, axis=0) - onehot
    rank_in = jnp.sum(before * onehot, axis=1)
    return flat_ids * capacity + rank_in


def body(residual, targets, block_ids, encoder_weight, encoder_bias, decoder_weight, decoder_bias):
    layer_index = lax.axis_index("layer")
    layers = lax.axis_size("layer")
    tok_count = lax.axis_size("tok")
    tok_rows = residual.shape[1]
    width = residual.shape[2]
    topk = block_ids.shape[2]
    per_owner = encoder_weight.shape[2] // BLOCK
    blocks = per_owner * tok_count
    capacity = max(2, 2 * tok_rows * topk // blocks)
    slot_count = blocks * capacity
    positions = jax.vmap(lambda ids: slot_positions(ids, blocks, capacity))(block_ids)
    own_positions = lax.dynamic_index_in_dim(positions, layer_index, 0, keepdims=False)
    source_row = (
        jnp.full((slot_count,), tok_rows, jnp.int32)
        .at[own_positions]
        .set(jnp.arange(tok_rows * topk, dtype=jnp.int32) // topk)
    )
    padded = jnp.concatenate([residual[0], jnp.zeros((1, width), residual.dtype)], axis=0)
    outgoing = padded[source_row].reshape(tok_count, per_owner * capacity, width)
    arrived = lax.all_to_all(outgoing, "tok", split_axis=0, concat_axis=0, tiled=True)
    arrived = arrived.reshape(tok_count, per_owner, capacity, width)
    enc_blocks = encoder_weight[0].reshape(width, per_owner, BLOCK)
    pre = jnp.einsum("sbcd,dbe->sbce", arrived, enc_blocks, preferred_element_type=jnp.float32)
    pre = pre + encoder_bias[0].reshape(per_owner, BLOCK)[None, :, None, :]
    codes = (
        jnp.maximum(pre, 0.0)
        .astype(jnp.bfloat16)
        .reshape(1, tok_count, per_owner * capacity, BLOCK)
    )
    all_codes = lax.all_gather(codes, "layer", axis=0, tiled=True)
    sources = jnp.arange(layers, dtype=jnp.int32)
    valid = sources <= layer_index
    weights = decoder_weight[0]
    keep_slot = valid.astype(jnp.float32)
    slot_sets = sources.shape[0]
    chosen_codes = (
        jnp.take(all_codes, sources, axis=0) * valid.astype(jnp.bfloat16)[:, None, None, None]
    )
    terms = (
        jnp.einsum(
            "snbce,sbed->snbcd",
            chosen_codes.reshape(slot_sets, tok_count, per_owner, capacity, BLOCK),
            weights.reshape(slot_sets, per_owner, BLOCK, width),
            preferred_element_type=jnp.float32,
        )
        .astype(jnp.bfloat16)
        .reshape(slot_sets, tok_count, per_owner * capacity, width)
    )
    returned = lax.all_to_all(terms, "tok", split_axis=1, concat_axis=1, tiled=True).reshape(
        slot_sets, slot_count, width
    )
    source_positions = jnp.take(positions, sources, axis=0)
    picked = jax.vmap(lambda rows, where_at: rows[where_at])(returned, source_positions)
    parts = jnp.sum(picked.astype(jnp.float32).reshape(slot_sets, tok_rows, topk, width), axis=2)
    own_sum = jnp.sum(parts * keep_slot[:, None, None], axis=0)
    recon32 = decoder_bias[0][None, :] + own_sum
    difference = recon32 - targets[0].astype(jnp.float32)
    error = jnp.mean(difference * difference, axis=1)
    return (recon32.astype(jnp.bfloat16)[None], error[None])


def solution(mesh):
    in_specs = (
        P("layer", "tok", None),
        P("layer", "tok", None),
        P(None, "tok", None),
        P("layer", None, "tok"),
        P("layer", "tok"),
        P("layer", None, "tok", None),
        P("layer", None),
    )
    out_specs = (P("layer", "tok", None), P("layer", "tok"))
    return jax.shard_map(body, mesh=mesh, in_specs=in_specs, out_specs=out_specs, check_vma=False)
```

profile of v0, /device:TPU:0, one launch (start us, length us, event | category | flops | bytes accessed | tf_op | source)
XLA Modules:
  0.0 584.5 jit_solution(2805510803366540468)
XLA Ops:
  0.6 0.8 copy.34
  1.5 1.0 copy.38
  2.5 0.9 fusion.14
  3.4 0.2 broadcast_add_fusion
  3.7 0.1 copy.35
  3.8 0.4 fusion.16
  4.2 1.4 scatter_custom_fusion
  5.6 1.2 concatenate.3
  6.9 4.2 gather_fusion
  11.1 6.3 %all-to-all-start = ((bf16[8,64,3584]{2,1,0:T(8,128)(2,1)}), bf16[8,64,3584]{2,1,0:T(8,128)(2,1)}, u32[]{:S(2)}, u32[]{:S(2)}) async-start(bf16[8,64,3584]{2,1,0:T(8,128)(2,1)} %bitcast.60), calls=%async_computation | async-start | bytes 7340032 | tf_op jit(solution)/shard_map/all_to_all | solution.py:37
  17.4 14.5 %copy.50 = bf16[448,8,16,128]{3,2,1,0:T(8,128)(2,1)} copy(bf16[448,8,16,128]{3,1,2,0:T(8,128)(2,1)} %bitcast.61) | data formatting | bytes 29360128
  31.9 0.0 copy-start.2
  31.9 68.3 %all-to-all-done = bf16[8,64,3584]{2,1,0:T(8,128)(2,1)} async-done(((bf16[8,64,3584]{2,1,0:T(8,128)(2,1)}), bf16[8,64,3584]{2,1,0:T(8,128)(2,1)}, u32[]{:S(2)}, u32[]{:S(2)}) %all-to-all-start) | async-done | bytes 3670048 | tf_op jit(solution)/shard_map/all_to_all | solution.py:37
  100.3 4.1 copy.40
  104.3 0.0 copy-done.2
  104.3 13.2 %fusion.11 = bf16[16,8,4,128]{3,1,2,0:T(8,128)(2,1)S(1)} fusion(bf16[8,16,4,3584]{3,0,2,1:T(8,128)(2,1)S(1)} %bitcast.63, bf16[3584,16,128,1]{2,1,0,3:T(8,128)(2,1)} %bitcast.62, f32[16,128]{1,0:T(8,128)S(1)} %bitcast.70), kind=kOutput, calls=%fused_computation.16 | convolution fusion | flops 469958656 | bytes 18489344 | tf_op jit(solution)/shard_map/sbcd,dbe->sbce/dot_general | solution.py:40
  117.6 10.2 %all_gather.3 = bf16[4,8,64,128]{3,2,1,0:T(8,128)(2,1)S(1)} all-gather(bf16[1,8,64,128]{3,2,1,0:T(8,128)(2,1)S(1)} %copy.42), channel_id=1, replica_groups=mesh['layer'=4,'tok'=8] {'layer'}, dimensions={0}, use_global_device_ids=true | all-gather | bytes 655360 | tf_op jit(solution)/shard_map/all_gather | solution.py:47
  127.8 0.6 gather_fusion.1
  128.5 25.9 %convolution_convert_fusion = bf16[4,16,8,4,3584]{4,2,3,1,0:T(8,128)(2,1)} fusion(bf16[4,16,128,3584,1]{3,2,4,1,0:T(8,128)(2,1)} %bitcast.59, bf16[4,8,16,4,128]{4,3,2,1,0:T(4,128)(2,1)S(1)} %bitcast.64, pred[4]{0:T(512)(128)(4,1)S(1)} %get-tuple-element.3, bf16[4]{0:T(256)(128)(2,1)S(1)} %get-tuple-element.2), kind=kOutput, calls=%fused_computation.7 | convolution fusion | flops 1886912512 | bytes 73924624 | tf_op jit(solution)/shard_map/snbce,sbed->snbcd/dot_general | solution.py:57
  154.4 15.6 %copy.44 = bf16[4,8,64,3584]{3,2,0,1:T(8,128)(2,1)} copy(bf16[4,8,64,3584]{3,1,2,0:T(8,128)(2,1)} %bitcast.58) | data formatting | bytes 29360128 | tf_op jit(solution)/shard_map/reshape | solution.py:64
  170.0 0.0 copy-start.1
  170.0 5.7 all-to-all-start.1
  175.7 0.6 gather_fusion.2
  176.2 0.1 fusion.27
  176.3 0.0 copy-done.1
  176.4 318.0 %all-to-all-done.1 = bf16[4,8,64,3584]{3,2,0,1:T(8,128)(2,1)} async-done(((bf16[4,8,64,3584]{3,2,0,1:T(8,128)(2,1)}), bf16[4,8,64,3584]{3,2,0,1:T(8,128)(2,1)}, u32[]{:S(2)}, u32[]{:S(2)}) %all-to-all-start.1) | async-done | bytes 14680096 | tf_op jit(solution)/shard_map/all_to_all | solution.py:66
  494.4 13.4 %copy.45 = bf16[4,8,64,3584]{3,2,1,0:T(8,128)(2,1)} copy(bf16[4,8,64,3584]{3,2,0,1:T(8,128)(2,1)} %all-to-all-done.1) | data formatting | bytes 29360128 | tf_op jit(solution)/shard_map/all_to_all | solution.py:66
  507.8 32.0 %gather_fusion.3 = bf16[1024,3584]{1,0:T(8,128)(2,1)} fusion(bf16[4,512,3584]{2,1,0:T(8,128)(2,1)} %bitcast.56, s32[1024]{0:T(1024)S(1)} %bitcast.57), kind=kCustom, calls=%fused_computation.3 | custom fusion | bytes 14688256 | tf_op jit(solution)/shard_map/vmap()/gather | solution.py:70
  539.8 16.2 %reshape.172 = f32[4,128,2,3584]{3,2,1,0:T(2,128)} reshape(bf16[1024,3584]{1,0:T(8,128)(2,1)} %gather_fusion.3) | data formatting | bytes 22020096 | tf_op jit(solution)/shard_map/convert_element_type | solution.py:71
  556.0 22.3 %reduce_sum.39 = f32[4,128,3584]{2,1,0:T(8,128)} reduce(f32[4,128,2,3584]{3,2,1,0:T(2,128)} %reshape.172, f32[]{:T(128)} %constant.75.clone.1), dimensions={2}, to_apply=%region_4.5 | reduce | flops 1835008 | bytes 22020100 | tf_op jit(solution)/shard_map/reduce_sum | solution.py:71
  578.3 0.0 copy-start
  578.3 4.3 multiply_reduce_fusion
  582.6 1.0 fusion.4
  583.6 0.0 copy-done
  583.6 0.4 fusion.3
  584.0 0.5 multiply_bitcast_fusion
  (16 shorter events, 0.2 us)
Async XLA Ops:
  11.1 89.2 %all-to-all-start = ((bf16[8,64,3584]{2,1,0:T(8,128)(2,1)}), bf16[8,64,3584]{2,1,0:T(8,128)(2,1)}, u32[]{:S(2)}, u32[]{:S(2)}) async-start(bf16[8,64,3584]{2,1,0:T(8,128)(2,1)} %bitcast.60), calls=%async_computation | async-start | bytes 7340032 | tf_op jit(solution)/shard_map/all_to_all | solution.py:37
  31.9 72.4 %copy-start.2 = (f32[1,2048]{1,0:T(1,128)S(1)}, f32[1,2048]{1,0:T(1,128)}, u32[]{:S(2)}) copy-start(f32[1,2048]{1,0:T(1,128)} %param.11) | copy-start | bytes 24580
  170.0 6.3 %copy-start.1 = (f32[1,3584]{1,0:T(1,128)S(1)}, f32[1,3584]{1,0:T(1,128)}, u32[]{:S(2)}) copy-start(f32[1,3584]{1,0:T(1,128)} %param.13) | copy-start | bytes 43012
  170.0 324.4 %all-to-all-start.1 = ((bf16[4,8,64,3584]{3,2,0,1:T(8,128)(2,1)}), bf16[4,8,64,3584]{3,2,0,1:T(8,128)(2,1)}, u32[]{:S(2)}, u32[]{:S(2)}) async-start(bf16[4,8,64,3584]{3,2,0,1:T(8,128)(2,1)} %copy.44), calls=%async_computation.1 | async-start | bytes 29360128 | tf_op jit(solution)/shard_map/all_to_all | solution.py:66
  578.3 5.3 copy-start
where the time goes:
time: 586 us; the launch traced here: 585 us
  waiting for transfers between devices  386 us (66%)
  local copies, waits for them, and re-layouts  106 us (18%)
  matrix products  39.1 us (7%)
  other arithmetic  30.2 us (5%)
  starting transfers between devices  12 us (2%)
  blocking collectives  10.2 us (2%)
    all_to_all x1, waiting for transfers between devices, body(): lax.all_to_all(terms, 'tok', split_axis=1, concat_axis=1, tiled=True)  318 us
    all_to_all x1, waiting for transfers between devices, body(): lax.all_to_all(outgoing, 'tok', split_axis=0, concat_axis=0, tiled=True)  68.3 us
    gather x1, local copies, waits for them, and re-layouts, body(): rows[where_at]  32 us
    dot_general x1, matrix products, body(): jnp.einsum('snbce,sbed->snbcd', chosen_codes.reshape(slot_sets, tok_count...  25.9 us
    reduce_sum x1, other arithmetic, body(): jnp.sum(picked.astype(jnp.float32).reshape(slot_sets, tok_rows, topk, wid...  22.3 us
    convert_element_type x1, local copies, waits for them, and re-layouts, body(): picked.astype(jnp.float32).reshape(slot_sets, tok_rows, topk, width)  16.2 us
    reshape x1, local copies, waits for them, and re-layouts, body(): terms = jnp.einsum('snbce,sbed->snbcd', chosen_codes.reshape(slot_sets, t...  15.6 us
    unnamed x9, local copies, waits for them, and re-layouts  15.3 us
  transfers between devices with their start and end apart: 2, of which 2 were waited for; matrix products, arithmetic and copies ran while one was open for 3% of the time, Pallas kernels for 0%

commit v1 on v0

--- a/solution.py
+++ b/solution.py
@@ -4,6 +4,22 @@
 from jax.sharding import PartitionSpec as P
 
 BLOCK = 128
+
+
+def swapped_with_each(x, axis, split, join):
+    ways, here = (lax.axis_size(axis), lax.axis_index(axis))
+    width = x.shape[split] // ways
+    lengths = list(x.shape)
+    lengths[split] = width
+    height = lengths[join]
+    lengths[join] = height * ways
+    full = jnp.zeros(lengths, x.dtype)
+    for mask in range(ways):
+        part = lax.dynamic_slice_in_dim(x, (here ^ mask) * width, width, axis=split)
+        if mask:
+            part = lax.ppermute(part, axis, [(d, d ^ mask) for d in range(ways)])
+        full = lax.dynamic_update_slice_in_dim(full, part, (here ^ mask) * height, axis=join)
+    return full
 
 
 def slot_positions(ids, blocks, capacity):
@@ -63,9 +79,7 @@
         .astype(jnp.bfloat16)
         .reshape(slot_sets, tok_count, per_owner * capacity, width)
     )
-    returned = lax.all_to_all(terms, "tok", split_axis=1, concat_axis=1, tiled=True).reshape(
-        slot_sets, slot_count, width
-    )
+    returned = swapped_with_each(terms, "tok", 1, 1).reshape(slot_sets, slot_count, width)
     source_positions = jnp.take(positions, sources, axis=0)
     picked = jax.vmap(lambda rows, where_at: rows[where_at])(returned, source_positions)
     parts = jnp.sum(picked.astype(jnp.float32).reshape(slot_sets, tok_rows, topk, width), axis=2)

time: 586 us -> 612 us (1.044)
  the two profiles are of different devices: /device:TPU:0 before, /device:TPU:11 now
where the time goes in v1:
time: 612 us; the launch traced here: 611 us
  waiting for transfers between devices  349 us (57%)
  local copies, waits for them, and re-layouts  166 us (27%)
  matrix products  39.2 us (6%)
  other arithmetic  30.2 us (5%)
  starting transfers between devices  17.2 us (3%)
  blocking collectives  8.25 us (1%)
    ppermute x7, waiting for transfers between devices, swapped_with_each(): part = lax.ppermute(part, axis, [(d, d ^ mask) for d in range(ways)])  284 us
    all_to_all x1, waiting for transfers between devices, body(): lax.all_to_all(outgoing, 'tok', split_axis=0, concat_axis=0, tiled=True)  64.7 us
    dynamic_slice x1, local copies, waits for them, and re-layouts, swapped_with_each(): part = lax.dynamic_slice_in_dim(x, (here ^ mask) * width, width, axis=split)  50.2 us
    gather x1, local copies, waits for them, and re-layouts, body(): rows[where_at]  31.9 us
    unnamed x26, local copies, waits for them, and re-layouts  29.3 us
    dot_general x1, matrix products, body(): jnp.einsum('snbce,sbed->snbcd', chosen_codes.reshape(slot_sets, tok_count...  25.9 us
    reduce_sum x1, other arithmetic, body(): jnp.sum(picked.astype(jnp.float32).reshape(slot_sets, tok_rows, topk, wid...  22.3 us
    dynamic_update_slice x8, local copies, waits for them, and re-layouts, swapped_with_each(): lax.dynamic_update_slice_in_dim(full, part, (here ^ mask) * height, axis=...  19.4 us
  transfers between devices with their start and end apart: 8, of which 6 were waited for; matrix products, arithmetic and copies ran while one was open for 8% of the time, Pallas kernels for 0%

profile of v1, /device:TPU:11, one launch (start us, length us, event | category | flops | bytes accessed | tf_op | source)
XLA Modules:
  0.0 610.7 jit_solution(2666494704854561816)
XLA Ops:
  0.7 0.9 copy.54
  1.6 1.0 copy.58
  2.6 0.9 fusion.14
  3.8 0.4 fusion.16
  4.3 1.4 scatter_custom_fusion
  5.8 4.2 gather_fusion
  10.0 5.6 all-to-all-start
  15.6 14.5 %copy.83 = bf16[448,8,16,128]{3,2,1,0:T(8,128)(2,1)} copy(bf16[448,8,16,128]{3,1,2,0:T(8,128)(2,1)} %bitcast.63) | data formatting | bytes 29360128
  30.2 64.7 %all-to-all-done = bf16[8,64,3584]{2,1,0:T(8,128)(2,1)} async-done(((bf16[8,64,3584]{2,1,0:T(8,128)(2,1)}), bf16[8,64,3584]{2,1,0:T(8,128)(2,1)}, u32[]{:S(2)}, u32[]{:S(2)}) %all-to-all-start) | async-done | bytes 3670048 | tf_op jit(solution)/shard_map/all_to_all | solution.py:53
  94.9 4.1 copy.60
  98.9 13.2 %fusion.11 = bf16[16,8,4,128]{3,1,2,0:T(8,128)(2,1)S(1)} fusion(bf16[8,16,4,3584]{3,0,2,1:T(8,128)(2,1)S(1)} %bitcast.65, bf16[3584,16,128,1]{2,1,0,3:T(8,128)(2,1)} %bitcast.64, f32[16,128]{1,0:T(8,128)S(1)} %bitcast.72), kind=kOutput, calls=%fused_computation.17 | convolution fusion | flops 469958656 | bytes 18489344 | tf_op jit(solution)/shard_map/sbcd,dbe->sbce/dot_general | solution.py:56
  112.2 8.3 %all_gather.3 = bf16[4,8,64,128]{3,2,1,0:T(8,128)(2,1)S(1)} all-gather(bf16[1,8,64,128]{3,2,1,0:T(8,128)(2,1)S(1)} %copy.62), channel_id=1, replica_groups=mesh['layer'=4,'tok'=8] {'layer'}, dimensions={0}, use_global_device_ids=true | all-gather | bytes 655360 | tf_op jit(solution)/shard_map/all_gather | solution.py:63
  120.4 0.6 gather_fusion.1
  121.1 25.9 %convolution_convert_fusion = bf16[4,16,8,4,3584]{4,2,3,1,0:T(8,128)(2,1)} fusion(bf16[4,16,128,3584,1]{3,2,4,1,0:T(8,128)(2,1)} %bitcast.61, bf16[4,8,16,4,128]{4,3,2,1,0:T(4,128)(2,1)S(1)} %bitcast.66, pred[4]{0:T(512)(128)(4,1)S(1)} %get-tuple-element.11, bf16[4]{0:T(256)(128)(2,1)S(1)} %get-tuple-element.10), kind=kOutput, calls=%fused_computation.7 | convolution fusion | flops 1886912512 | bytes 73924624 | tf_op jit(solution)/shard_map/snbce,sbed->snbcd/dot_general | solution.py:73
  147.0 50.2 %constant_dynamic-slice_fusion = (bf16[4,1,64,3584]{3,1,2,0:T(2,128)(2,1)}, bf16[4,1,64,3584]{3,1,2,0:T(2,128)(2,1)}, bf16[4,1,64,3584]{3,1,2,0:T(2,128)(2,1)}, ...) fusion(bf16[4,8,64,3584]{3,1,2,0:T(8,128)(2,1)} %bitcast.59, ...), kind=kLoop, calls=%fused_computation.36 | loop fusion | bytes 29360160 | tf_op jit(solution)/shard_map/dynamic_slice | solution.py:18
  197.2 1.5 copy.76
  198.6 2.5 collective-permute-start
  201.1 0.6 gather_fusion.2
  201.7 3.5 copy.77
  205.2 3.5 collective-permute-start.1
  208.8 3.7 copy.78
  212.5 1.5 copy.79
  214.0 1.2 collective-permute-start.3
  215.3 1.5 copy.80
  216.7 1.7 collective-permute-start.4
  218.4 6.9 %broadcast_in_dim.37 = bf16[4,8,64,3584]{3,2,1,0:T(8,128)(2,1)} broadcast(bf16[]{:T(256)} %constant.38.clone.1), dimensions={} | broadcast | bytes 14680066 | tf_op jit(solution)/shard_map/broadcast_in_dim | solution.py:16
  225.3 3.7 copy_dynamic-update-slice_fusion
  229.2 1.8 copy-done
  231.4 2.9 constant_dynamic-update-slice_fusion.6
  234.3 84.3 %collective-permute-done.1 = bf16[4,1,64,3584]{3,2,1,0:T(8,128)(2,1)S(1)} collective-permute-done((bf16[4,1,64,3584]{3,2,1,0:T(8,128)(2,1)}, bf16[4,1,64,3584]{3,2,1,0:T(8,128)(2,1)S(1)}, u32[]{:S(2)}, u32[]{:S(2)}) %collective-permute-start.1) | collective-permute-done | bytes 1835040 | tf_op jit(solution)/shard_map/ppermute | solution.py:20
  318.6 2.6 collective-permute-start.6
  321.2 1.3 constant_dynamic-update-slice_fusion.5
  322.5 35.4 %collective-permute-done.2 = bf16[4,1,64,3584]{3,2,1,0:T(8,128)(2,1)} collective-permute-done((bf16[4,1,64,3584]{3,2,1,0:T(8,128)(2,1)}, bf16[4,1,64,3584]{3,2,1,0:T(8,128)(2,1)}, u32[]{:S(2)}, u32[]{:S(2)}) %collective-permute-start.2) | collective-permute-done | bytes 1835040 | tf_op jit(solution)/shard_map/ppermute | solution.py:20
  357.9 2.9 constant_dynamic-update-slice_fusion.4
  360.8 2.9 constant_dynamic-update-slice_fusion.3
  363.7 87.7 %collective-permute-done.4 = bf16[4,1,64,3584]{3,2,1,0:T(8,128)(2,1)} collective-permute-done((bf16[4,1,64,3584]{3,2,1,0:T(8,128)(2,1)}, bf16[4,1,64,3584]{3,2,1,0:T(8,128)(2,1)}, u32[]{:S(2)}, u32[]{:S(2)}) %collective-permute-start.4) | collective-permute-done | bytes 1835040 | tf_op jit(solution)/shard_map/ppermute | solution.py:20
  451.4 2.8 constant_dynamic-update-slice_fusion.2
  454.3 38.7 %collective-permute-done.5 = bf16[4,1,64,3584]{3,2,1,0:T(8,128)(2,1)S(1)} collective-permute-done((bf16[4,1,64,3584]{3,2,1,0:T(8,128)(2,1)S(1)}, bf16[4,1,64,3584]{3,2,1,0:T(8,128)(2,1)S(1)}, u32[]{:S(2)}, u32[]{:S(2)}) %collective-permute-start.5) | collective-permute-done | bytes 1835040 | tf_op jit(solution)/shard_map/ppermute | solution.py:20
  493.0 1.4 constant_dynamic-update-slice_fusion.1
  494.4 38.3 %collective-permute-done.6 = bf16[4,1,64,3584]{3,2,1,0:T(8,128)(2,1)S(1)} collective-permute-done((bf16[4,1,64,3584]{3,2,1,0:T(8,128)(2,1)S(1)}, bf16[4,1,64,3584]{3,2,1,0:T(8,128)(2,1)S(1)}, u32[]{:S(2)}, u32[]{:S(2)}) %collective-permute-start.6) | collective-permute-done | bytes 1835040 | tf_op jit(solution)/shard_map/ppermute | solution.py:20
  532.6 1.4 constant_dynamic-update-slice_fusion
  534.1 31.9 %gather_fusion.3 = bf16[1024,3584]{1,0:T(8,128)(2,1)} fusion(bf16[4,512,3584]{2,1,0:T(8,128)(2,1)} %bitcast.58, s32[1024]{0:T(1024)S(1)} %bitcast.60), kind=kCustom, calls=%fused_computation.3 | custom fusion | bytes 14688256 | tf_op jit(solution)/shard_map/vmap()/gather | solution.py:84
  566.0 16.2 %reshape.172 = f32[4,128,2,3584]{3,2,1,0:T(2,128)} reshape(bf16[1024,3584]{1,0:T(8,128)(2,1)} %gather_fusion.3) | data formatting | bytes 22020096 | tf_op jit(solution)/shard_map/convert_element_type | solution.py:85
  582.1 22.3 %reduce_sum.39 = f32[4,128,3584]{2,1,0:T(8,128)} reduce(f32[4,128,2,3584]{3,2,1,0:T(2,128)} %reshape.172, f32[]{:T(128)} %constant.85.clone.1), dimensions={2}, to_apply=%region_4.5 | reduce | flops 1835008 | bytes 22020100 | tf_op jit(solution)/shard_map/reduce_sum | solution.py:85
  604.5 4.3 multiply_reduce_fusion
  608.7 1.0 fusion.4
  609.8 0.4 fusion.3
  610.2 0.5 multiply_bitcast_fusion
  (41 shorter events, 1.2 us)
Async XLA Ops:
  0.6 5.1 copy-start.4
  10.0 84.9 %all-to-all-start = ((bf16[8,64,3584]{2,1,0:T(8,128)(2,1)}), bf16[8,64,3584]{2,1,0:T(8,128)(2,1)}, u32[]{:S(2)}, u32[]{:S(2)}) async-start(bf16[8,64,3584]{2,1,0:T(8,128)(2,1)} %bitcast.62), calls=%async_computation | async-start | bytes 7340032 | tf_op jit(solution)/shard_map/all_to_all | solution.py:53
  30.2 68.8 %copy-start.7 = (f32[1,2048]{1,0:T(1,128)S(1)}, f32[1,2048]{1,0:T(1,128)}, u32[]{:S(2)}) copy-start(f32[1,2048]{1,0:T(1,128)} %param.11) | copy-start | bytes 24580
  198.6 10.1 %copy-start.6 = (f32[1,3584]{1,0:T(1,128)S(1)}, f32[1,3584]{1,0:T(1,128)}, u32[]{:S(2)}) copy-start(f32[1,3584]{1,0:T(1,128)} %param.13) | copy-start | bytes 43012
  198.6 32.6 %collective-permute-start = (bf16[4,1,64,3584]{3,2,1,0:T(8,128)(2,1)}, bf16[4,1,64,3584]{3,2,1,0:T(8,128)(2,1)}, u32[]{:S(2)}, u32[]{:S(2)}) collective-permute-start(bf16[4,1,64,3584]{3,2,1,0:T(8,128)(2,1)} %copy.76), channel_id=1, source_target_pairs={{0,1},{1,0},{2,3},{3,2},{4,5},{5,4},{6,7},{7,6},{8,9},{9,8},{10,11... | collective-permute-start | bytes 5505032 | tf_op jit(solution)/shard_map/ppermute | solution.py:20
  205.2 113.4 %collective-permute-start.1 = (bf16[4,1,64,3584]{3,2,1,0:T(8,128)(2,1)}, bf16[4,1,64,3584]{3,2,1,0:T(8,128)(2,1)S(1)}, u32[]{:S(2)}, u32[]{:S(2)}) collective-permute-start(bf16[4,1,64,3584]{3,2,1,0:T(8,128)(2,1)} %copy.77), channel_id=1, source_target_pairs={{0,2},{1,3},{2,0},{3,1},{4,6},{5,7},{6,4},{7,5},{8,10},{9,11},{10,... | collective-permute-start | bytes 5505032 | tf_op jit(solution)/shard_map/ppermute | solution.py:20
  208.8 3.7 copy-start.3
  212.5 2.7 copy-start.2
  212.5 145.4 %collective-permute-start.2 = (bf16[4,1,64,3584]{3,2,1,0:T(8,128)(2,1)}, bf16[4,1,64,3584]{3,2,1,0:T(8,128)(2,1)}, u32[]{:S(2)}, u32[]{:S(2)}) collective-permute-start(bf16[4,1,64,3584]{3,2,1,0:T(8,128)(2,1)} %copy.78), channel_id=1, source_target_pairs={{0,3},{1,2},{2,1},{3,0},{4,7},{5,6},{6,5},{7,4},{8,11},{9,10},{10,... | collective-permute-start | bytes 5505032 | tf_op jit(solution)/shard_map/ppermute | solution.py:20
  214.0 146.8 %collective-permute-start.3 = (bf16[4,1,64,3584]{3,2,1,0:T(8,128)(2,1)}, bf16[4,1,64,3584]{3,2,1,0:T(8,128)(2,1)}, u32[]{:S(2)}, u32[]{:S(2)}) collective-permute-start(bf16[4,1,64,3584]{3,2,1,0:T(8,128)(2,1)} %copy.79), channel_id=1, source_target_pairs={{0,4},{1,5},{2,6},{3,7},{4,0},{5,1},{6,2},{7,3},{8,12},{9,13},{10,... | collective-permute-start | bytes 5505032 | tf_op jit(solution)/shard_map/ppermute | solution.py:20
  216.7 234.7 %collective-permute-start.4 = (bf16[4,1,64,3584]{3,2,1,0:T(8,128)(2,1)}, bf16[4,1,64,3584]{3,2,1,0:T(8,128)(2,1)}, u32[]{:S(2)}, u32[]{:S(2)}) collective-permute-start(bf16[4,1,64,3584]{3,2,1,0:T(8,128)(2,1)} %copy.80), channel_id=1, source_target_pairs={{0,5},{1,4},{2,7},{3,6},{4,1},{5,0},{6,3},{7,2},{8,13},{9,12},{10,... | collective-permute-start | bytes 5505032 | tf_op jit(solution)/shard_map/ppermute | solution.py:20
  225.3 3.7 copy-start.1
  229.0 2.0 copy-start
  231.3 261.7 %collective-permute-start.5 = (bf16[4,1,64,3584]{3,2,1,0:T(8,128)(2,1)S(1)}, bf16[4,1,64,3584]{3,2,1,0:T(8,128)(2,1)S(1)}, u32[]{:S(2)}, u32[]{:S(2)}) collective-permute-start(bf16[4,1,64,3584]{3,2,1,0:T(8,128)(2,1)S(1)} %copy.81), channel_id=1, source_target_pairs={{0,6},{1,7},{2,4},{3,5},{4,2},{5,3},{6,0},{7,1},{8,14},{9,15},{10,... | collective-permute-start | bytes 5505032 | tf_op jit(solution)/shard_map/ppermute | solution.py:20
  318.6 214.1 %collective-permute-start.6 = (bf16[4,1,64,3584]{3,2,1,0:T(8,128)(2,1)S(1)}, bf16[4,1,64,3584]{3,2,1,0:T(8,128)(2,1)S(1)}, u32[]{:S(2)}, u32[]{:S(2)}) collective-permute-start(bf16[4,1,64,3584]{3,2,1,0:T(8,128)(2,1)S(1)} %copy.82), channel_id=1, source_target_pairs={{0,7},{1,6},{2,5},{3,4},{4,3},{5,2},{6,1},{7,0},{8,15},{9,14},{10,... | collective-permute-start | bytes 5505032 | tf_op jit(solution)/shard_map/ppermute | solution.py:20
  604.5 5.3 copy-start.5
